TPU v7x, 32 devices: a whole 2x2x4 slice. The times are simulated.
32 devices in a mesh: space: 16 (over z, y, x), ray: 2 (over core).
Axes of the slice: x: 2, y: 2, z: 4, core: 2. Of those that a mesh axis runs over, the one named last changes fastest.
Arguments:
- positions: float32 [3, 512, 256], P(None, ('space', 'ray')), may hold values from -1 to 1
- spacing: float32 [512, 256], P(('space', 'ray')), may hold values from 0.003 to 0.03
- assign: int32 [512, 8, 1], P(('space', 'ray')), may hold values from 0 to 15; in each aligned block of 128 rows (0 to 127, 128 to 255, ..., all dimensions but the last counted through in order) at most 12 rows name the same one
- depth_rank: int32 [512, 8], P(('space', 'ray')), may hold values from 0 to 7, each once within a row
- pixel_grad: float32 [3, 512], P(None, ('space', 'ray')), may hold values from -96 to 96
- fourier: float32 [3, 128], replicated, may hold values from -4 to 4
- first_weight: bfloat16 [16, 256, 256], P('space'), may hold values from -0.375 to 0.375
- first_bias: float32 [16, 256], P('space'), may hold values from -3 to 3
- second_weight: bfloat16 [16, 256, 256], P('space'), may hold values from -0.375 to 0.375
- second_bias: float32 [16, 256], P('space'), may hold values from -3 to 3
- head_weight: bfloat16 [16, 4, 256], P('space'), may hold values from -0.375 to 0.375
- head_bias: float32 [16, 4], P('space'), may hold values from -3 to 3
Outputs:
- grad_first: float32 [16, 256, 256], P('space', 'ray')
- grad_second: float32 [16, 256, 256], P('space', 'ray')
- grad_head: float32 [16, 4, 256], P('space')
- grad_first_bias: float32 [16, 256], P('space')
- grad_second_bias: float32 [16, 256], P('space')
- grad_head_bias: float32 [16, 4], P('space')
Inputs may be any that keep to these rules, and one draw needn't show every extreme that they name: `assign`: within the segments of one device (aligned blocks of 128 rows in ray order), no partition is named more than 12 times. `depth_rank`: each ray's row names every place 0 to 7 once.
All inputs are finite; a program needn't handle non-finite values.
Results may differ from a plain program's by a relative error of at most 0.0053.
Values sent between devices are 32-bit elements; how exact they have to be, the bound alone decides.
No kernel may reach another device: no remote copies, remote signals or barrier semaphores. Data moves between devices by JAX's collectives and lax.ppermute only.
A program may use at most 64 MiB of HBM per device.

v0:
```python
import jax
import jax.numpy as jnp
from jax import lax
from jax.sharding import PartitionSpec as P

SEG_LEN = 32
SEGS = 8
two_pi = 6.283185307179586


def silu_slope(value):
    gate = jax.nn.sigmoid(value)
    return gate * (1.0 + value * (1.0 - gate))


def turn_sin_cos(turns):
    quarter = jnp.round(turns * 4.0)
    angle = (turns - quarter * 0.25) * two_pi
    square = angle * angle
    sine = angle * (
        1.0
        + square
        * (
            -1.0 / 6.0
            + square * (1.0 / 120.0 + square * (-1.0 / 5040.0 + square * (1.0 / 362880.0)))
        )
    )
    cosine = 1.0 + square * (
        -0.5
        + square
        * (
            1.0 / 24.0
            + square * (-1.0 / 720.0 + square * (1.0 / 40320.0 + square * (-1.0 / 3628800.0)))
        )
    )
    step = quarter - 4.0 * jnp.floor(quarter * 0.25)
    flip = step >= 2.0
    odd = (step == 1.0) | (step == 3.0)
    sin_out = jnp.where(odd, cosine, sine)
    cos_out = jnp.where(odd, sine, cosine)
    sin_out = jnp.where(flip, -sin_out, sin_out)
    cos_out = jnp.where(flip != odd, -cos_out, cos_out)
    return (sin_out, cos_out)


def encode(samples, fourier):
    turns = (
        samples[:, 0, :, None] * fourier[0]
        + samples[:, 1, :, None] * fourier[1]
        + samples[:, 2, :, None] * fourier[2]
    )
    sine, cosine = turn_sin_cos(turns)
    joined = jnp.concatenate([sine, cosine], axis=-1)
    return joined.astype(jnp.bfloat16).reshape(-1, joined.shape[-1])


def network(samples, fourier, params):
    first_weight, first_bias, second_weight, second_bias, head_weight, head_bias = params
    seg_count, length = (samples.shape[0], samples.shape[2])
    encoded = encode(samples, fourier)
    pre_first = jnp.dot(encoded, first_weight, preferred_element_type=jnp.float32) + first_bias
    act_first = jax.nn.silu(pre_first).astype(jnp.bfloat16)
    pre_second = jnp.dot(act_first, second_weight, preferred_element_type=jnp.float32) + second_bias
    act_second = jax.nn.silu(pre_second).astype(jnp.bfloat16)
    head_raw = (
        lax.dot_general(
            act_second, head_weight, (((1,), (1,)), ((), ())), preferred_element_type=jnp.float32
        )
        + head_bias
    )
    head_raw = head_raw.reshape(seg_count, length, 4)
    density = jax.nn.softplus(head_raw[..., 0])
    colour = jax.nn.sigmoid(head_raw[..., 1:])
    optical = density * samples[:, 3, :]
    inclusive = jnp.cumsum(optical, axis=1)
    enter_light = jnp.exp(optical - inclusive)
    leave_light = jnp.exp(-inclusive)
    weight = enter_light - leave_light
    seg_colour = jnp.sum(weight[..., None] * colour, axis=1)
    seg_log = -inclusive[:, -1]
    saved = (
        encoded,
        pre_first,
        act_first,
        pre_second,
        act_second,
        head_raw,
        colour,
        weight,
        leave_light,
    )
    return (seg_colour, seg_log, saved)


def backward(samples, params, saved, up_colour, up_log):
    first_weight, first_bias, second_weight, second_bias, head_weight, head_bias = params
    encoded, pre_first, act_first, pre_second, act_second, head_raw, colour, weight, leave_light = (
        saved
    )
    energy = jnp.sum(colour * up_colour[:, None, :], axis=-1)
    spent = weight * energy
    remaining = jnp.sum(spent, axis=1, keepdims=True) - jnp.cumsum(spent, axis=1)
    grad_optical = leave_light * energy - remaining - up_log[:, None]
    grad_density = grad_optical * samples[:, 3, :] * jax.nn.sigmoid(head_raw[..., 0])
    grad_tint = weight[..., None] * up_colour[:, None, :] * colour * (1.0 - colour)
    grad_raw = (
        jnp.concatenate([grad_density[..., None], grad_tint], axis=-1)
        .reshape(-1, 4)
        .astype(jnp.bfloat16)
    )
    grad_head = lax.dot_general(
        grad_raw, act_second, (((0,), (0,)), ((), ())), preferred_element_type=jnp.float32
    )
    grad_head_bias = jnp.sum(grad_raw.astype(jnp.float32), axis=0)
    back_second = jnp.dot(grad_raw, head_weight, preferred_element_type=jnp.float32)
    delta_second = (back_second * silu_slope(pre_second)).astype(jnp.bfloat16)
    grad_second = lax.dot_general(
        act_first, delta_second, (((0,), (0,)), ((), ())), preferred_element_type=jnp.float32
    )
    grad_second_bias = jnp.sum(delta_second.astype(jnp.float32), axis=0)
    back_first = lax.dot_general(
        delta_second, second_weight, (((1,), (1,)), ((), ())), preferred_element_type=jnp.float32
    )
    delta_first = (back_first * silu_slope(pre_first)).astype(jnp.bfloat16)
    grad_first = lax.dot_general(
        encoded, delta_first, (((0,), (0,)), ((), ())), preferred_element_type=jnp.float32
    )
    grad_first_bias = jnp.sum(delta_first.astype(jnp.float32), axis=0)
    return (grad_first, grad_second, grad_head, grad_first_bias, grad_second_bias, grad_head_bias)


def composite(seg_colour, seg_log, depth_rank, pixel_rows):
    before = (depth_rank[:, None, :] < depth_rank[:, :, None]).astype(jnp.float32)
    prefix = jnp.exp(jnp.sum(before * seg_log[:, None, :], axis=2))
    up_colour = prefix[..., None] * pixel_rows[:, None, :]
    shaded = prefix * jnp.sum(seg_colour * pixel_rows[:, None, :], axis=2)
    up_log = jnp.sum(before * shaded[:, :, None], axis=1)
    return (up_colour, up_log)


def per_device(
    positions,
    spacing,
    assign,
    depth_rank,
    pixel_grad,
    fourier,
    first_weight,
    first_bias,
    second_weight,
    second_bias,
    head_weight,
    head_bias,
):
    groups = lax.axis_size("space")
    ray_count = positions.shape[1]
    total = ray_count * SEGS
    capacity = 3 * total // (2 * groups)
    slot_count = capacity * groups
    owner = assign.reshape(total)
    member = (owner[:, None] == jnp.arange(groups, dtype=jnp.int32)[None, :]).astype(jnp.int32)
    earlier = jnp.cumsum(member, axis=0) - member
    within = jnp.sum(earlier * member, axis=1)
    target = owner * capacity + within
    dispatch = (target[:, None] == jnp.arange(slot_count, dtype=jnp.int32)[None, :]).astype(
        jnp.float32
    )
    seg_pos = jnp.transpose(positions.reshape(3, total, SEG_LEN), (1, 0, 2))
    seg_gap = spacing.reshape(total, 1, SEG_LEN)
    segments = jnp.concatenate([seg_pos, seg_gap], axis=1).reshape(total, 4 * SEG_LEN)
    outgoing = lax.dot_general(
        dispatch,
        segments,
        (((0,), (0,)), ((), ())),
        precision=lax.Precision.HIGHEST,
        preferred_element_type=jnp.float32,
    )
    outgoing = outgoing.reshape(groups, capacity, 4 * SEG_LEN)
    arrived = lax.all_to_all(outgoing, "space", split_axis=0, concat_axis=0, tiled=True)
    samples = arrived.reshape(slot_count, 4, SEG_LEN)
    params = tuple(
        (
            item[0]
            for item in (
                first_weight,
                first_bias,
                second_weight,
                second_bias,
                head_weight,
                head_bias,
            )
        )
    )
    seg_colour, seg_log, saved = network(samples, fourier, params)
    partials = jnp.concatenate([seg_colour.T, seg_log[None, :]], axis=0).reshape(
        4, groups, capacity
    )
    returned = lax.all_to_all(partials, "space", split_axis=1, concat_axis=1, tiled=True).reshape(
        4, slot_count
    )
    mine = lax.dot_general(
        dispatch,
        returned,
        (((1,), (1,)), ((), ())),
        precision=lax.Precision.HIGHEST,
        preferred_element_type=jnp.float32,
    )
    up_colour, up_log = composite(
        mine[:, :3].reshape(ray_count, SEGS, 3),
        mine[:, 3].reshape(ray_count, SEGS),
        depth_rank,
        pixel_grad.T,
    )
    upstream = jnp.concatenate([up_colour.reshape(total, 3), up_log.reshape(total, 1)], axis=1)
    sendback = lax.dot_general(
        upstream,
        dispatch,
        (((0,), (0,)), ((), ())),
        precision=lax.Precision.HIGHEST,
        preferred_element_type=jnp.float32,
    )
    sendback = sendback.reshape(4, groups, capacity)
    received = lax.all_to_all(sendback, "space", split_axis=1, concat_axis=1, tiled=True)
    received = received.reshape(4, slot_count).T
    totals = backward(samples, params, saved, received[:, :3], received[:, 3])
    grad_first, grad_second, grad_head, bias_first, bias_second, bias_head = totals
    replicas = lax.axis_size("ray")
    small = jnp.concatenate([grad_head.reshape(-1), bias_first, bias_second, bias_head], axis=0)
    if replicas & replicas - 1 == 0:
        position = lax.axis_index("ray")
        part_first, part_second = (grad_first, grad_second)
        distance = replicas // 2
        while distance >= 1:
            pairs = [(i, i ^ distance) for i in range(replicas)]
            half = part_first.shape[0] // 2
            upper = position // distance % 2
            keep_first = lax.dynamic_slice_in_dim(part_first, upper * half, half, 0)
            send_first = lax.dynamic_slice_in_dim(part_first, (1 - upper) * half, half, 0)
            keep_second = lax.dynamic_slice_in_dim(part_second, upper * half, half, 0)
            send_second = lax.dynamic_slice_in_dim(part_second, (1 - upper) * half, half, 0)
            got_first, got_second, got_small = lax.ppermute(
                (send_first, send_second, small), "ray", pairs
            )
            part_first = keep_first + got_first
            part_second = keep_second + got_second
            small = small + got_small
            distance //= 2
    else:
        part_first = lax.psum_scatter(grad_first, "ray", scatter_dimension=0, tiled=True)
        part_second = lax.psum_scatter(grad_second, "ray", scatter_dimension=0, tiled=True)
        small = lax.psum(small, "ray")
    heads = grad_head.size
    hidden = bias_first.shape[0]
    small_sums = (
        small[:heads].reshape(grad_head.shape),
        small[heads : heads + hidden],
        small[heads + hidden : heads + 2 * hidden],
        small[heads + 2 * hidden :],
    )
    return (
        part_first[None],
        part_second[None],
        small_sums[0][None],
        small_sums[1][None],
        small_sums[2][None],
        small_sums[3][None],
    )


def solution(mesh):
    placed = (
        P(None, ("space", "ray"), None),
        P(("space", "ray"), None),
        P(("space", "ray"), None, None),
        P(("space", "ray"), None),
        P(None, ("space", "ray")),
        P(),
        P("space", None, None),
        P("space", None),
        P("space", None, None),
        P("space", None),
        P("space", None, None),
        P("space", None),
    )
    return jax.shard_map(
        per_device,
        mesh=mesh,
        in_specs=placed,
        out_specs=(
            P("space", "ray", None),
            P("space", "ray", None),
            P("space", None, None),
            P("space", None),
            P("space", None),
            P("space", None),
        ),
        check_vma=False,
    )
```

profile of v0, /device:TPU:1, one launch (start us, length us, event | category | flops | bytes accessed | tf_op | source)
XLA Modules:
  0.0 90.0 jit_solution(858286756958283039)
XLA Ops:
  0.7 0.8 copy.53
  1.5 0.1 reshape.233
  1.5 0.1 fusion.25
  1.6 0.2 reduce_window_sum.30
  1.8 0.2 select_reduce_fusion
  2.0 0.9 reshape.234
  2.9 0.1 copy.54
  3.0 0.8 reshape.235
  3.9 0.1 broadcast_compare_fusion.1
  4.0 0.9 fusion.21
  4.9 7.4 %all-to-all-start = ((f32[16,12,128]{2,1,0:T(8,128)}), f32[16,12,128]{2,1,0:T(8,128)S(1)}, u32[]{:S(2)}, u32[]{:S(2)}) async-start(f32[16,12,128]{2,1,0:T(8,128)} %fusion.21), calls=%async_computation | async-start | bytes 262144 | tf_op jit(solution)/shard_map/all_to_all | solution.py:179
  12.3 0.8 slice_bitcast_fusion.3
  13.1 5.8 %all-to-all-done = f32[16,12,128]{2,1,0:T(8,128)S(1)} async-done(((f32[16,12,128]{2,1,0:T(8,128)}), f32[16,12,128]{2,1,0:T(8,128)S(1)}, u32[]{:S(2)}, u32[]{:S(2)}) %all-to-all-start) | async-done | bytes 98336 | tf_op jit(solution)/shard_map/all_to_all | solution.py:179
  19.0 0.2 reshape.237
  19.2 0.9 %slice_reduce_fusion.2 = (f32[192,32]{1,0:T(8,128)S(1)}, f32[192,32]{1,0:T(8,128)S(1)}, f32[192,32]{1,0:T(8,128)S(1)}, f32[192,1,32]{2,1,0:T(1,128)S(1)}) fusion(f32[192,4,32]{2,1,0:T(4,128)S(1)} %reshape.237), kind=kLoop, calls=%fused_computation.61 | loop fusion | bytes 196608 | tf_op jit(solution)/shard_map/slice | solution.py:48
  20.1 0.1 mul.309
  20.2 0.1 mul.314
  20.3 0.1 mul.319
  20.4 5.6 %fusion.2 = (bf16[6144,128]{1,0:T(8,128)(2,1)S(1)}, bf16[6144,128]{1,0:T(8,128)(2,1)S(1)}) fusion(f32[128]{0:T(128)S(1)} %get-tuple-element.19, f32[6144]{0:T(1024)S(1)} %mul.319, f32[128]{0:T(128)S(1)} %get-tuple-element.20, f32[6144]{0:T(1024)S(1)} %mul.314, f32[128]{0:T(128)S(1)} %get-tuple-element.18, f32[6144]{0:T(1024)S(1)} %mul.309), kind=kLoop, calls=%fused_computation.15 | loop fusion | flops 36175872 | bytes 3220992 | tf_op jit(solution)/shard_map/convert.4
  26.1 4.7 %multiply_convert_fusion.1 = (bf16[6144,256]{1,0:T(8,128)(2,1)S(1)}, f32[6144,256]{1,0:T(8,128)}) fusion(f32[256]{0:T(256)S(1)} %bitcast.134, bf16[1,256,256]{2,1,0:T(8,128)(2,1)} %param.18, bf16[6144,128]{1,0:T(8,128)(2,1)S(1)} %get-tuple-element.13, bf16[6144,128]{1,0:T(8,128)(2,1)S(1)} %get-tuple-element.12), kind=kOutput, calls=%fused_computation.11 | convolution fusion | flops 821035008 | bytes 12715008 | tf_op jit(solution)/shard_map/dot_general | solution.py:61
  30.9 4.4 %multiply_convert_fusion = (bf16[6144,256]{1,0:T(8,128)(2,1)S(1)}, f32[6144,256]{1,0:T(8,128)}) fusion(f32[256]{0:T(256)S(1)} %bitcast.135, bf16[6144,256]{1,0:T(8,128)(2,1)S(1)} %get-tuple-element.21, bf16[1,256,256]{2,1,0:T(8,128)(2,1)S(1)} %copy-done), kind=kOutput, calls=%fused_computation.9 | convolution fusion | flops 814743552 | bytes 12715008 | tf_op jit(solution)/shard_map/dot_general | solution.py:63
  35.3 0.9 %convolution_add_fusion.2 = f32[6144,4]{0,1:T(4,128)S(1)} fusion(bf16[6144,256]{1,0:T(8,128)(2,1)S(1)} %get-tuple-element.23, f32[4]{0:T(128)S(1)} %bitcast.130, bf16[1,4,256]{2,1,0:T(4,128)(2,1)S(1)} %copy-done.6), kind=kOutput, calls=%fused_computation.6 | convolution fusion | flops 12607488 | bytes 3246096 | tf_op jit(solution)/shard_map/dot_general | solution.py:66
  36.2 0.9 %reshape.238 = f32[192,32,4]{1,0,2:T(8,128)} reshape(f32[6144,4]{0,1:T(4,128)S(1)} %convolution_add_fusion.2) | data formatting | bytes 196608 | tf_op jit(solution)/shard_map/reshape | solution.py:71
  37.1 0.9 slice.77
  38.3 0.1 copy.60
  38.4 1.2 %multiply_reduce_fusion.1 = f32[192,3]{0,1:T(4,128)S(1)} fusion(f32[192,32]{1,0:T(8,128)S(1)} %copy.60, f32[192,32,4]{1,0,2:T(8,128)} %reshape.238), kind=kLoop, calls=%fused_computation.48 | loop fusion | flops 91584 | bytes 100608 | tf_op jit(solution)/shard_map/reduce_sum | solution.py:79
  39.6 0.1 concatenate.31
  39.8 0.6 copy.61
  40.4 3.5 %all-to-all-start.1 = ((f32[4,16,12]{2,0,1:T(4,128)}), f32[4,16,12]{2,0,1:T(4,128)S(1)}, u32[]{:S(2)}, u32[]{:S(2)}) async-start(f32[4,16,12]{2,0,1:T(4,128)} %copy.61), calls=%async_computation.1 | async-start | bytes 65536 | tf_op jit(solution)/shard_map/all_to_all | solution.py:198
  43.9 0.7 mul.353
  44.6 0.8 mul.354
  45.4 4.7 %all-to-all-done.1 = f32[4,16,12]{2,0,1:T(4,128)S(1)} async-done(((f32[4,16,12]{2,0,1:T(4,128)}), f32[4,16,12]{2,0,1:T(4,128)S(1)}, u32[]{:S(2)}, u32[]{:S(2)}) %all-to-all-start.1) | async-done | bytes 3104 | tf_op jit(solution)/shard_map/all_to_all | solution.py:198
  50.1 0.6 copy.62
  50.8 0.8 reshape.239
  51.6 0.8 fusion.20
  52.8 0.1 copy.63
  53.0 0.1 exp.69
  53.2 0.1 reshape.240
  53.3 0.9 fusion.19
  54.1 0.1 reshape.241
  54.3 0.6 copy.67
  54.9 3.7 %all-to-all-start.2 = ((f32[4,16,12]{2,0,1:T(4,128)}), f32[4,16,12]{2,0,1:T(4,128)S(1)}, u32[]{:S(2)}, u32[]{:S(2)}) async-start(f32[4,16,12]{2,0,1:T(4,128)} %copy.67), calls=%async_computation.2 | async-start | bytes 65536 | tf_op jit(solution)/shard_map/all_to_all | solution.py:223
  58.6 6.0 %all-to-all-done.2 = f32[4,16,12]{2,0,1:T(4,128)S(1)} async-done(((f32[4,16,12]{2,0,1:T(4,128)}), f32[4,16,12]{2,0,1:T(4,128)S(1)}, u32[]{:S(2)}, u32[]{:S(2)}) %all-to-all-start.2) | async-done | bytes 3104 | tf_op jit(solution)/shard_map/all_to_all | solution.py:223
  64.6 0.6 copy.68
  65.2 0.8 reshape.242
  66.1 2.4 %multiply_reduce_fusion = (f32[192,32]{1,0:T(8,128)}, bf16[192,32,3]{1,0,2:T(8,128)(2,1)}) fusion(f32[192,3]{0,1:T(4,128)S(1)} %bitcast.126, f32[192,32,4]{1,0,2:T(8,128)} %reshape.238, f32[192,32]{1,0:T(8,128)S(1)} %copy.60), kind=kLoop, calls=%fused_computation.47 | loop fusion | flops 178176 | bytes 162048 | tf_op jit(solution)/shard_map/reduce_sum | solution.py:100
  68.5 1.0 %copy.69 = f32[192,32]{0,1:T(8,128)S(1)} copy(f32[192,32]{1,0:T(8,128)} %get-tuple-element.9) | data formatting | bytes 49152 | tf_op jit(solution)/shard_map/reduce_sum | solution.py:100
  69.7 0.1 copy.71
  69.8 0.1 concatenate.34
  69.9 1.1 %concatenate.35 = bf16[6144,3]{0,1:T(4,128)(2,1)S(1)} reshape(bf16[192,32,3]{1,0,2:T(8,128)(2,1)} %get-tuple-element.10) | data formatting | bytes 73728 | tf_op jit(solution)/shard_map/concatenate | solution.py:107
  71.0 0.5 convolution_bitcast_fusion
  71.5 0.2 convert_reduce_fusion.2
  71.7 5.2 %convert_reduce_fusion = (f32[256]{0:T(256)S(1)}, bf16[6144,256]{1,0:T(8,128)(2,1)S(1)}) fusion(f32[6144,256]{1,0:T(8,128)} %get-tuple-element.24, bf16[1,4,256]{2,1,0:T(4,128)(2,1)S(1)} %copy-done.6, bf16[6144,3]{0,1:T(4,128)(2,1)S(1)} %concatenate.35, bf16[6144,1]{0,1:T(2,128)(2,1)S(1)} %concatenate.34), kind=kOutput, calls=%fused_computation.7 | convolution fusion | flops 29982464 | bytes 9489408 | tf_op jit(solution)/shard_map/dot_general | solution.py:115
  76.9 1.0 %fusion.56 = f32[256,256]{1,0:T(8,128)S(1)} fusion(bf16[6144,256]{1,0:T(8,128)(2,1)S(1)} %copy-done.13, bf16[6144,256]{1,0:T(8,128)(2,1)S(1)} %get-tuple-element.26), kind=kOutput, calls=%fused_computation.126 | convolution fusion | flops 805306368 | bytes 6553600 | tf_op jit(solution)/shard_map/dot_general | solution.py:117
  78.0 2.8 %convert_reduce_fusion.1 = (f32[256]{0:T(256)S(1)}, bf16[6144,256]{1,0:T(8,128)(2,1)S(1)}) fusion(f32[6144,256]{1,0:T(8,128)S(1)} %bitcast.137, bf16[6144,256]{1,0:T(8,128)(2,1)S(1)} %get-tuple-element.26, bf16[1,256,256]{2,1,0:T(8,128)(2,1)S(1)} %copy-done), kind=kOutput, calls=%fused_computation.8 | convolution fusion | flops 822607616 | bytes 12715008 | tf_op jit(solution)/shard_map/dot_general | solution.py:121
  80.8 4.5 %collective-permute-start.2 = (f32[1540]{0:T(1024)S(1)}, f32[1540]{0:T(1024)S(1)}, u32[]{:S(2)}, u32[]{:S(2)}) collective-permute-start(f32[1540]{0:T(1024)S(1)} %pad_maximum_fusion.6), channel_id=1, source_target_pairs={{0,1},{1,0},{2,3},{3,2},{4,5},{5,4},{6,7},{7,6},{8,9},{9,8},{10,11... | collective-permute-start | bytes 18488 | tf_op jit(solution)/shard_map/ppermute | solution.py:241
  85.3 0.1 collective-permute-start.1
  85.4 1.0 %fusion.12 = f32[256,256]{1,0:T(8,128)S(1)} fusion(bf16[6144,256]{1,0:T(8,128)(2,1)S(1)} %get-tuple-element.28, bf16[6144,128]{1,0:T(8,128)(2,1)S(1)} %copy-done.4, bf16[6144,128]{1,0:T(8,128)(2,1)S(1)} %copy-done.2), kind=kOutput, calls=%fused_computation.39 | convolution fusion | flops 811597824 | bytes 6553600 | tf_op jit(solution)/shard_map/dot_general | solution.py:125
  86.4 0.5 collective-permute-start
  87.0 0.6 fusion.54
  87.6 0.6 broadcast_in_dim_reshape.4
  88.2 0.5 slice_bitcast_fusion
  88.7 0.7 add_bitcast_fusion
  89.4 0.7 add_bitcast_fusion.1
  (70 shorter events, 1.3 us)
Async XLA Ops:
  0.6 30.2 %copy-start = (bf16[1,256,256]{2,1,0:T(8,128)(2,1)S(1)}, bf16[1,256,256]{2,1,0:T(8,128)(2,1)}, u32[]{:S(2)}) copy-start(bf16[1,256,256]{2,1,0:T(8,128)(2,1)} %param.20) | copy-start | bytes 393220
  1.8 24.3 %copy-start.10 = (f32[1,256]{1,0:T(1,128)S(1)}, f32[1,256]{1,0:T(1,128)}, u32[]{:S(2)}) copy-start(f32[1,256]{1,0:T(1,128)} %param.19) | copy-start | bytes 3076
  2.0 17.0 %copy-start.9 = (s32[128]{0:T(128)}, s32[128]{0:T(128)S(1)}, u32[]{:S(2)}) copy-start(s32[128]{0:T(128)S(1)} %multiply_add_fusion.2) | copy-start | bytes 1540
  4.9 14.1 %all-to-all-start = ((f32[16,12,128]{2,1,0:T(8,128)}), f32[16,12,128]{2,1,0:T(8,128)S(1)}, u32[]{:S(2)}, u32[]{:S(2)}) async-start(f32[16,12,128]{2,1,0:T(8,128)} %fusion.21), calls=%async_computation | async-start | bytes 262144 | tf_op jit(solution)/shard_map/all_to_all | solution.py:179
  26.1 4.8 %copy-start.1 = (bf16[6144,128]{1,0:T(8,128)(2,1)}, bf16[6144,128]{1,0:T(8,128)(2,1)S(1)}, u32[]{:S(2)}) copy-start(bf16[6144,128]{1,0:T(8,128)(2,1)S(1)} %get-tuple-element.12) | copy-start | bytes 4718596
  26.1 4.8 %copy-start.3 = (bf16[6144,128]{1,0:T(8,128)(2,1)}, bf16[6144,128]{1,0:T(8,128)(2,1)S(1)}, u32[]{:S(2)}) copy-start(bf16[6144,128]{1,0:T(8,128)(2,1)S(1)} %get-tuple-element.13) | copy-start | bytes 4718596
  26.1 4.8 %copy-start.11 = (f32[1,256]{1,0:T(1,128)S(1)}, f32[1,256]{1,0:T(1,128)}, u32[]{:S(2)}) copy-start(f32[1,256]{1,0:T(1,128)} %param.21) | copy-start | bytes 3076
  30.8 4.4 %copy-start.12 = (bf16[6144,256]{1,0:T(8,128)(2,1)}, bf16[6144,256]{1,0:T(8,128)(2,1)S(1)}, u32[]{:S(2)}) copy-start(bf16[6144,256]{1,0:T(8,128)(2,1)S(1)} %get-tuple-element.21) | copy-start | bytes 9437188
  30.9 4.4 %copy-start.6 = (bf16[1,4,256]{2,1,0:T(4,128)(2,1)S(1)}, bf16[1,4,256]{2,1,0:T(4,128)(2,1)}, u32[]{:S(2)}) copy-start(bf16[1,4,256]{2,1,0:T(4,128)(2,1)} %param.22) | copy-start | bytes 6148
  30.9 4.4 %copy-start.7 = (f32[1,4]{1,0:T(1,128)S(1)}, f32[1,4]{1,0:T(1,128)}, u32[]{:S(2)}) copy-start(f32[1,4]{1,0:T(1,128)} %param.23) | copy-start | bytes 52
  35.3 8.7 %copy-start.8 = (f32[3,16]{1,0:T(4,128)S(1)}, f32[3,16]{1,0:T(4,128)}, u32[]{:S(2)}) copy-start(f32[3,16]{1,0:T(4,128)} %param.16) | copy-start | bytes 580
  35.3 17.6 %copy-start.5 = (s32[16,8]{0,1:T(8,128)S(1)}, s32[16,8]{0,1:T(8,128)}, u32[]{:S(2)}) copy-start(s32[16,8]{0,1:T(8,128)} %param.15) | copy-start | bytes 1540
  40.4 9.7 %all-to-all-start.1 = ((f32[4,16,12]{2,0,1:T(4,128)}), f32[4,16,12]{2,0,1:T(4,128)S(1)}, u32[]{:S(2)}, u32[]{:S(2)}) async-start(f32[4,16,12]{2,0,1:T(4,128)} %copy.61), calls=%async_computation.1 | async-start | bytes 65536 | tf_op jit(solution)/shard_map/all_to_all | solution.py:198
  54.9 9.7 %all-to-all-start.2 = ((f32[4,16,12]{2,0,1:T(4,128)}), f32[4,16,12]{2,0,1:T(4,128)S(1)}, u32[]{:S(2)}, u32[]{:S(2)}) async-start(f32[4,16,12]{2,0,1:T(4,128)} %copy.67), calls=%async_computation.2 | async-start | bytes 65536 | tf_op jit(solution)/shard_map/all_to_all | solution.py:223
  71.0 7.0 %slice-start = ((s8[6291456]{0:T(1024)(128)(4,1)}), s8[4194304]{0:T(1024)(128)(4,1)S(1)}, s32[]{:S(2)}) async-start(s8[6291456]{0:T(1024)(128)(4,1)} %bitcast.136), calls=%async_computation.3 | async-start | bytes 8388608
  71.7 5.2 %copy-start.13 = (bf16[6144,256]{1,0:T(8,128)(2,1)S(1)}, bf16[6144,256]{1,0:T(8,128)(2,1)}, u32[]{:S(2)}) copy-start(bf16[6144,256]{1,0:T(8,128)(2,1)} %copy-done.12) | copy-start | bytes 9437188
  71.7 6.2 %slice-start.1 = ((s8[6291456]{0:T(1024)(128)(4,1)}), s8[2097152]{0:T(1024)(128)(4,1)S(1)}, s32[]{:S(2)}) async-start(s8[6291456]{0:T(1024)(128)(4,1)} %bitcast.136), calls=%async_computation.4 | async-start | bytes 4194304
  78.0 7.4 %copy-start.2 = (bf16[6144,128]{1,0:T(8,128)(2,1)S(1)}, bf16[6144,128]{1,0:T(8,128)(2,1)}, u32[]{:S(2)}) copy-start(bf16[6144,128]{1,0:T(8,128)(2,1)} %copy-done.1) | copy-start | bytes 4718596
  78.0 7.4 %copy-start.4 = (bf16[6144,128]{1,0:T(8,128)(2,1)S(1)}, bf16[6144,128]{1,0:T(8,128)(2,1)}, u32[]{:S(2)}) copy-start(bf16[6144,128]{1,0:T(8,128)(2,1)} %copy-done.3) | copy-start | bytes 4718596
  80.8 6.2 %collective-permute-start.2 = (f32[1540]{0:T(1024)S(1)}, f32[1540]{0:T(1024)S(1)}, u32[]{:S(2)}, u32[]{:S(2)}) collective-permute-start(f32[1540]{0:T(1024)S(1)} %pad_maximum_fusion.6), channel_id=1, source_target_pairs={{0,1},{1,0},{2,3},{3,2},{4,5},{5,4},{6,7},{7,6},{8,9},{9,8},{10,11... | collective-permute-start | bytes 18488 | tf_op jit(solution)/shard_map/ppermute | solution.py:241
  85.3 3.4 %collective-permute-start.1 = (f32[128,256]{1,0:T(8,128)S(1)}, f32[128,256]{1,0:T(8,128)S(1)}, u32[]{:S(2)}, u32[]{:S(2)}) collective-permute-start(f32[128,256]{1,0:T(8,128)S(1)} %constant_dynamic-slice_fusion.1), channel_id=1, source_target_pairs={{0,1},{1,0},{2,3},{3,2},{4,5},{5,4},{6,7},{7,6},{8,9},{9,8},{10,11... | collective-permute-start | bytes 393224 | tf_op jit(solution)/shard_map/ppermute | solution.py:241
  86.4 2.9 %collective-permute-start = (f32[128,256]{1,0:T(8,128)S(1)}, f32[128,256]{1,0:T(8,128)S(1)}, u32[]{:S(2)}, u32[]{:S(2)}) collective-permute-start(f32[128,256]{1,0:T(8,128)S(1)} %constant_dynamic-slice_fusion), channel_id=1, source_target_pairs={{0,1},{1,0},{2,3},{3,2},{4,5},{5,4},{6,7},{7,6},{8,9},{9,8},{10,11... | collective-permute-start | bytes 393224 | tf_op jit(solution)/shard_map/ppermute | solution.py:241
where the time goes:
time: 90.9 us; the launch traced here: 90 us
  matrix products  23.1 us (25%)
  starting transfers between devices  19.7 us (22%)
  local copies, waits for them, and re-layouts  17.7 us (19%)
  waiting for transfers between devices  16.6 us (18%)
  other arithmetic  11.7 us (13%)
  between operations  1.15 us (1%)
    all_to_all x1, starting transfers between devices, per_device(): lax.all_to_all(outgoing, 'space', split_axis=0, concat_axis=0, tiled=True)  7.41 us
    all_to_all x1, waiting for transfers between devices, per_device(): lax.all_to_all(sendback, 'space', split_axis=1, concat_axis=1, tiled=True)  6.02 us
    all_to_all x1, waiting for transfers between devices, per_device(): lax.all_to_all(outgoing, 'space', split_axis=0, concat_axis=0, tiled=True)  5.85 us
    another operation x2, other arithmetic  5.68 us
    dot_general x1, matrix products, backward(): jnp.dot(grad_raw, head_weight, preferred_element_type=jnp.float32)  5.17 us
    ppermute x3, starting transfers between devices, per_device(): lax.ppermute((send_first, send_second, small), 'ray', pairs)  5.1 us
    dot_general x1, matrix products, network(): jnp.dot(encoded, first_weight, preferred_element_type=jnp.float32)  4.73 us
    all_to_all x1, waiting for transfers between devices, per_device(): lax.all_to_all(partials, 'space', split_axis=1, concat_axis=1, tiled=True)  4.71 us
  transfers between devices with their start and end apart: 6, of which 3 were waited for; matrix products, arithmetic and copies ran while one was open for 6% of the time, Pallas kernels for 0%

commit v1 on v0

--- a/solution.py
+++ b/solution.py
@@ -220,7 +220,12 @@
         preferred_element_type=jnp.float32,
     )
     sendback = sendback.reshape(4, groups, capacity)
-    received = lax.all_to_all(sendback, "space", split_axis=1, concat_axis=1, tiled=True)
+    received = jnp.concatenate(
+        lax.all_to_all(
+            jnp.stack(jnp.split(sendback, lax.axis_size("space"), axis=1)), "space", 0, 0
+        ),
+        axis=1,
+    )
     received = received.reshape(4, slot_count).T
     totals = backward(samples, params, saved, received[:, :3], received[:, 3])
     grad_first, grad_second, grad_head, bias_first, bias_second, bias_head = totals

time: 90.9 us -> 98.4 us (1.083)
  local copies, waits for them, and re-layouts: 17.7 us -> 26.4 us
  matrix products: 23.1 us -> 22 us
    unnamed x36 -> x53, local copies, waits for them, and re-layouts: 1.02 us -> 9.7 us
    another operation x1 -> x3, local copies, waits for them, and re-layouts: 0.11 us -> 1.54 us  [the longest x1 0.84 us: per_device(): received = received.reshape(4, slot_count).T]
    dot_general x1, matrix products: 4.73 us -> 3.62 us  [network(): jnp.dot(encoded, first_weight, preferred_element_type=jnp.float32)]
where the time goes in v1:
time: 98.4 us; the launch traced here: 97.6 us
  local copies, waits for them, and re-layouts  26.4 us (27%)
  matrix products  22 us (22%)
  starting transfers between devices  19.7 us (20%)
  waiting for transfers between devices  16.6 us (17%)
  other arithmetic  11.7 us (12%)
  between operations  1.18 us (1%)
    unnamed x53, local copies, waits for them, and re-layouts  9.7 us
    all_to_all x1, starting transfers between devices, per_device(): lax.all_to_all(outgoing, 'space', split_axis=0, concat_axis=0, tiled=True)  7.42 us
    all_to_all x1, waiting for transfers between devices, per_device(): lax.all_to_all(jnp.stack(jnp.split(sendback, lax.axis_size('space'), axis...  6.02 us
    all_to_all x1, waiting for transfers between devices, per_device(): lax.all_to_all(outgoing, 'space', split_axis=0, concat_axis=0, tiled=True)  5.85 us
    another operation x2, other arithmetic  5.68 us
    dot_general x1, matrix products, backward(): jnp.dot(grad_raw, head_weight, preferred_element_type=jnp.float32)  5.18 us
    ppermute x3, starting transfers between devices, per_device(): lax.ppermute((send_first, send_second, small), 'ray', pairs)  5.11 us
    all_to_all x1, waiting for transfers between devices, per_device(): lax.all_to_all(partials, 'space', split_axis=1, concat_axis=1, tiled=True)  4.71 us
  transfers between devices with their start and end apart: 6, of which 3 were waited for; matrix products, arithmetic and copies ran while one was open for 6% of the time, Pallas kernels for 0%

profile of v1, /device:TPU:1, one launch (start us, length us, event | category | flops | bytes accessed | tf_op | source)
XLA Modules:
  0.0 97.6 jit_solution(4750769835178546444)
XLA Ops:
  0.7 0.8 copy.69
  1.6 0.2 reduce_window_sum.30
  1.8 0.2 select_reduce_fusion
  2.0 0.9 reshape.234
  3.0 0.8 reshape.235
  4.0 0.9 fusion.21
  4.9 7.4 %all-to-all-start = ((f32[16,12,128]{2,1,0:T(8,128)}), f32[16,12,128]{2,1,0:T(8,128)S(1)}, u32[]{:S(2)}, u32[]{:S(2)}) async-start(f32[16,12,128]{2,1,0:T(8,128)} %fusion.21), calls=%async_computation | async-start | bytes 262144 | tf_op jit(solution)/shard_map/all_to_all | solution.py:179
  12.3 0.8 slice_bitcast_fusion.3
  13.1 5.8 %all-to-all-done = f32[16,12,128]{2,1,0:T(8,128)S(1)} async-done(((f32[16,12,128]{2,1,0:T(8,128)}), f32[16,12,128]{2,1,0:T(8,128)S(1)}, u32[]{:S(2)}, u32[]{:S(2)}) %all-to-all-start) | async-done | bytes 98336 | tf_op jit(solution)/shard_map/all_to_all | solution.py:179
  19.0 0.2 reshape.237
  19.2 0.9 slice_reduce_fusion.2
  20.4 5.6 %fusion.2 = (bf16[6144,128]{1,0:T(8,128)(2,1)S(1)}, bf16[6144,128]{1,0:T(8,128)(2,1)S(1)}) fusion(f32[128]{0:T(128)S(1)} %get-tuple-element.35, f32[6144]{0:T(1024)S(1)} %mul.319, f32[128]{0:T(128)S(1)} %get-tuple-element.36, f32[6144]{0:T(1024)S(1)} %mul.314, f32[128]{0:T(128)S(1)} %get-tuple-element.34, f32[6144]{0:T(1024)S(1)} %mul.309), kind=kLoop, calls=%fused_computation.15 | loop fusion | flops 36175872 | bytes 3220992 | tf_op jit(solution)/shard_map/convert.4
  26.1 3.6 %multiply_convert_fusion.1 = (bf16[6144,256]{1,0:T(8,128)(2,1)S(1)}, f32[6144,256]{1,0:T(8,128)}) fusion(f32[256]{0:T(256)S(1)} %bitcast.172, bf16[1,256,256]{2,1,0:T(8,128)(2,1)S(1)} %copy-done.10, bf16[6144,128]{1,0:T(8,128)(2,1)S(1)} %get-tuple-element.13, bf16[6144,128]{1,0:T(8,128)(2,1)S(1)} %get-tuple-element.12), kind=kOutput, calls=%fused_computation.11 | convolution fusion | flops 821035008 | bytes 12715008 | tf_op jit(solution)/shard_map/dot_general | solution.py:61
  29.8 4.4 %multiply_convert_fusion = (bf16[6144,256]{1,0:T(8,128)(2,1)S(1)}, f32[6144,256]{1,0:T(8,128)}) fusion(f32[256]{0:T(256)S(1)} %bitcast.173, bf16[6144,256]{1,0:T(8,128)(2,1)S(1)} %get-tuple-element.37, bf16[1,256,256]{2,1,0:T(8,128)(2,1)S(1)} %copy-done), kind=kOutput, calls=%fused_computation.9 | convolution fusion | flops 814743552 | bytes 12715008 | tf_op jit(solution)/shard_map/dot_general | solution.py:63
  34.2 0.9 convolution_add_fusion.2
  35.1 0.9 reshape.238
  36.0 0.9 slice.77
  37.3 1.2 %multiply_reduce_fusion.1 = f32[192,3]{0,1:T(4,128)S(1)} fusion(f32[192,32]{1,0:T(8,128)S(1)} %copy.76, f32[192,32,4]{1,0,2:T(8,128)} %reshape.238), kind=kLoop, calls=%fused_computation.48 | loop fusion | flops 91584 | bytes 100608 | tf_op jit(solution)/shard_map/reduce_sum | solution.py:79
  38.7 0.6 copy.77
  39.3 3.5 %all-to-all-start.1 = ((f32[4,16,12]{2,0,1:T(4,128)}), f32[4,16,12]{2,0,1:T(4,128)S(1)}, u32[]{:S(2)}, u32[]{:S(2)}) async-start(f32[4,16,12]{2,0,1:T(4,128)} %copy.77), calls=%async_computation.1 | async-start | bytes 65536 | tf_op jit(solution)/shard_map/all_to_all | solution.py:198
  42.8 0.7 mul.353
  43.5 0.8 mul.354
  44.3 4.7 %all-to-all-done.1 = f32[4,16,12]{2,0,1:T(4,128)S(1)} async-done(((f32[4,16,12]{2,0,1:T(4,128)}), f32[4,16,12]{2,0,1:T(4,128)S(1)}, u32[]{:S(2)}, u32[]{:S(2)}) %all-to-all-start.1) | async-done | bytes 3104 | tf_op jit(solution)/shard_map/all_to_all | solution.py:198
  49.1 0.6 copy.78
  49.7 0.8 reshape.239
  50.5 0.8 fusion.20
  52.2 0.9 fusion.19
  53.0 0.1 reshape.241
  53.2 0.6 constant_dynamic-update-slice_fusion.15
  53.8 0.6 constant_dynamic-update-slice_fusion.14
  54.4 0.6 constant_dynamic-update-slice_fusion.13
  54.9 0.6 constant_dynamic-update-slice_fusion.12
  55.5 0.6 constant_dynamic-update-slice_fusion.11
  56.1 0.6 constant_dynamic-update-slice_fusion.10
  56.7 0.6 constant_dynamic-update-slice_fusion.9
  57.3 0.6 constant_dynamic-update-slice_fusion.8
  57.8 0.6 constant_dynamic-update-slice_fusion.7
  58.4 0.6 constant_dynamic-update-slice_fusion.6
  59.0 0.6 constant_dynamic-update-slice_fusion.5
  59.6 0.6 constant_dynamic-update-slice_fusion.4
  60.2 0.6 constant_dynamic-update-slice_fusion.3
  60.7 0.6 constant_dynamic-update-slice_fusion.2
  61.3 0.6 constant_dynamic-update-slice_fusion.1
  61.9 0.6 constant_dynamic-update-slice_fusion
  62.5 3.7 %all-to-all-start.2 = ((f32[16,4,1,12]{3,1,2,0:T(4,128)}), f32[16,4,1,12]{3,1,2,0:T(4,128)S(1)}, u32[]{:S(2)}, u32[]{:S(2)}) async-start(f32[16,4,1,12]{3,1,2,0:T(4,128)} %constant_dynamic-update-slice_fusion), calls=%async_computation.2 | async-start | bytes 65536 | tf_op jit(solution)/shard_map/all_to_all | solution.py:224
  66.2 6.0 %all-to-all-done.2 = f32[16,4,1,12]{3,1,2,0:T(4,128)S(1)} async-done(((f32[16,4,1,12]{3,1,2,0:T(4,128)}), f32[16,4,1,12]{3,1,2,0:T(4,128)S(1)}, u32[]{:S(2)}, u32[]{:S(2)}) %all-to-all-start.2) | async-done | bytes 3104 | tf_op jit(solution)/shard_map/all_to_all | solution.py:224
  72.2 0.6 copy.83
  72.8 0.8 reshape_reshape.3
  73.7 2.4 %multiply_reduce_fusion = (f32[192,32]{1,0:T(8,128)}, bf16[192,32,3]{1,0,2:T(8,128)(2,1)}) fusion(f32[192,3]{0,1:T(4,128)S(1)} %bitcast.148, f32[192,32,4]{1,0,2:T(8,128)} %reshape.238, f32[192,32]{1,0:T(8,128)S(1)} %copy.76), kind=kLoop, calls=%fused_computation.47 | loop fusion | flops 178176 | bytes 162048 | tf_op jit(solution)/shard_map/reduce_sum | solution.py:100
  76.1 1.0 copy.84
  77.5 1.1 %concatenate.35 = bf16[6144,3]{0,1:T(4,128)(2,1)S(1)} reshape(bf16[192,32,3]{1,0,2:T(8,128)(2,1)} %get-tuple-element.10) | data formatting | bytes 73728 | tf_op jit(solution)/shard_map/concatenate | solution.py:107
  78.6 0.5 convolution_bitcast_fusion
  79.1 0.2 convert_reduce_fusion.2
  79.3 5.2 %convert_reduce_fusion = (f32[256]{0:T(256)S(1)}, bf16[6144,256]{1,0:T(8,128)(2,1)S(1)}) fusion(f32[6144,256]{1,0:T(8,128)} %get-tuple-element.40, bf16[1,4,256]{2,1,0:T(4,128)(2,1)S(1)} %copy-done.6, bf16[6144,3]{0,1:T(4,128)(2,1)S(1)} %concatenate.35, bf16[6144,1]{0,1:T(2,128)(2,1)S(1)} %concatenate.34), kind=kOutput, calls=%fused_computation.7 | convolution fusion | flops 29982464 | bytes 9489408 | tf_op jit(solution)/shard_map/dot_general | solution.py:115
  84.5 1.0 %fusion.57 = f32[256,256]{1,0:T(8,128)S(1)} fusion(bf16[6144,256]{1,0:T(8,128)(2,1)S(1)} %copy-done.14, bf16[6144,256]{1,0:T(8,128)(2,1)S(1)} %get-tuple-element.42), kind=kOutput, calls=%fused_computation.143 | convolution fusion | flops 805306368 | bytes 6553600 | tf_op jit(solution)/shard_map/dot_general | solution.py:117
  85.6 2.7 %convert_reduce_fusion.1 = (f32[256]{0:T(256)S(1)}, bf16[6144,256]{1,0:T(8,128)(2,1)S(1)}) fusion(f32[6144,256]{1,0:T(8,128)S(1)} %bitcast.175, bf16[6144,256]{1,0:T(8,128)(2,1)S(1)} %get-tuple-element.42, bf16[1,256,256]{2,1,0:T(8,128)(2,1)S(1)} %copy-done), kind=kOutput, calls=%fused_computation.8 | convolution fusion | flops 822607616 | bytes 12715008 | tf_op jit(solution)/shard_map/dot_general | solution.py:121
  88.3 4.5 %collective-permute-start.2 = (f32[1540]{0:T(1024)S(1)}, f32[1540]{0:T(1024)S(1)}, u32[]{:S(2)}, u32[]{:S(2)}) collective-permute-start(f32[1540]{0:T(1024)S(1)} %pad_maximum_fusion.6), channel_id=1, source_target_pairs={{0,1},{1,0},{2,3},{3,2},{4,5},{5,4},{6,7},{7,6},{8,9},{9,8},{10,11... | collective-permute-start | bytes 18488 | tf_op jit(solution)/shard_map/ppermute | solution.py:246
  92.9 1.0 %fusion.12 = f32[256,256]{1,0:T(8,128)S(1)} fusion(bf16[6144,256]{1,0:T(8,128)(2,1)S(1)} %get-tuple-element.44, bf16[6144,128]{1,0:T(8,128)(2,1)S(1)} %copy-done.4, bf16[6144,128]{1,0:T(8,128)(2,1)S(1)} %copy-done.2), kind=kOutput, calls=%fused_computation.39 | convolution fusion | flops 811597824 | bytes 6553600 | tf_op jit(solution)/shard_map/dot_general | solution.py:125
  94.0 0.5 collective-permute-start
  94.5 0.6 fusion.55
  95.1 0.6 broadcast_in_dim_reshape.4
  95.7 0.5 slice_bitcast_fusion
  96.2 0.7 add_bitcast_fusion
  96.9 0.7 add_bitcast_fusion.1
  (88 shorter events, 2.7 us)
Async XLA Ops:
  0.6 29.1 %copy-start = (bf16[1,256,256]{2,1,0:T(8,128)(2,1)S(1)}, bf16[1,256,256]{2,1,0:T(8,128)(2,1)}, u32[]{:S(2)}) copy-start(bf16[1,256,256]{2,1,0:T(8,128)(2,1)} %param.20) | copy-start | bytes 393220
  1.8 24.3 %copy-start.10 = (bf16[1,256,256]{2,1,0:T(8,128)(2,1)S(1)}, bf16[1,256,256]{2,1,0:T(8,128)(2,1)}, u32[]{:S(2)}) copy-start(bf16[1,256,256]{2,1,0:T(8,128)(2,1)} %param.18) | copy-start | bytes 393220
  1.8 24.3 %copy-start.11 = (f32[1,256]{1,0:T(1,128)S(1)}, f32[1,256]{1,0:T(1,128)}, u32[]{:S(2)}) copy-start(f32[1,256]{1,0:T(1,128)} %param.19) | copy-start | bytes 3076
  2.0 17.0 %copy-start.9 = (s32[128]{0:T(128)}, s32[128]{0:T(128)S(1)}, u32[]{:S(2)}) copy-start(s32[128]{0:T(128)S(1)} %multiply_add_fusion.2) | copy-start | bytes 1540
  4.9 14.1 %all-to-all-start = ((f32[16,12,128]{2,1,0:T(8,128)}), f32[16,12,128]{2,1,0:T(8,128)S(1)}, u32[]{:S(2)}, u32[]{:S(2)}) async-start(f32[16,12,128]{2,1,0:T(8,128)} %fusion.21), calls=%async_computation | async-start | bytes 262144 | tf_op jit(solution)/shard_map/all_to_all | solution.py:179
  26.1 3.7 %copy-start.1 = (bf16[6144,128]{1,0:T(8,128)(2,1)}, bf16[6144,128]{1,0:T(8,128)(2,1)S(1)}, u32[]{:S(2)}) copy-start(bf16[6144,128]{1,0:T(8,128)(2,1)S(1)} %get-tuple-element.12) | copy-start | bytes 4718596
  26.1 3.7 %copy-start.3 = (bf16[6144,128]{1,0:T(8,128)(2,1)}, bf16[6144,128]{1,0:T(8,128)(2,1)S(1)}, u32[]{:S(2)}) copy-start(bf16[6144,128]{1,0:T(8,128)(2,1)S(1)} %get-tuple-element.13) | copy-start | bytes 4718596
  26.1 3.6 %copy-start.12 = (f32[1,256]{1,0:T(1,128)S(1)}, f32[1,256]{1,0:T(1,128)}, u32[]{:S(2)}) copy-start(f32[1,256]{1,0:T(1,128)} %param.21) | copy-start | bytes 3076
  29.7 4.4 %copy-start.13 = (bf16[6144,256]{1,0:T(8,128)(2,1)}, bf16[6144,256]{1,0:T(8,128)(2,1)S(1)}, u32[]{:S(2)}) copy-start(bf16[6144,256]{1,0:T(8,128)(2,1)S(1)} %get-tuple-element.37) | copy-start | bytes 9437188
  29.8 4.4 %copy-start.6 = (bf16[1,4,256]{2,1,0:T(4,128)(2,1)S(1)}, bf16[1,4,256]{2,1,0:T(4,128)(2,1)}, u32[]{:S(2)}) copy-start(bf16[1,4,256]{2,1,0:T(4,128)(2,1)} %param.22) | copy-start | bytes 6148
  29.8 4.4 %copy-start.7 = (f32[1,4]{1,0:T(1,128)S(1)}, f32[1,4]{1,0:T(1,128)}, u32[]{:S(2)}) copy-start(f32[1,4]{1,0:T(1,128)} %param.23) | copy-start | bytes 52
  34.2 8.7 %copy-start.8 = (f32[3,16]{1,0:T(4,128)S(1)}, f32[3,16]{1,0:T(4,128)}, u32[]{:S(2)}) copy-start(f32[3,16]{1,0:T(4,128)} %param.16) | copy-start | bytes 580
  34.2 17.6 %copy-start.5 = (s32[16,8]{0,1:T(8,128)S(1)}, s32[16,8]{0,1:T(8,128)}, u32[]{:S(2)}) copy-start(s32[16,8]{0,1:T(8,128)} %param.15) | copy-start | bytes 1540
  39.3 9.7 %all-to-all-start.1 = ((f32[4,16,12]{2,0,1:T(4,128)}), f32[4,16,12]{2,0,1:T(4,128)S(1)}, u32[]{:S(2)}, u32[]{:S(2)}) async-start(f32[4,16,12]{2,0,1:T(4,128)} %copy.77), calls=%async_computation.1 | async-start | bytes 65536 | tf_op jit(solution)/shard_map/all_to_all | solution.py:198
  62.5 9.7 %all-to-all-start.2 = ((f32[16,4,1,12]{3,1,2,0:T(4,128)}), f32[16,4,1,12]{3,1,2,0:T(4,128)S(1)}, u32[]{:S(2)}, u32[]{:S(2)}) async-start(f32[16,4,1,12]{3,1,2,0:T(4,128)} %constant_dynamic-update-slice_fusion), calls=%async_computation.2 | async-start | bytes 65536 | tf_op jit(solution)/shard_map/all_to_all | solution.py:224
  78.6 6.9 %slice-start = ((s8[6291456]{0:T(1024)(128)(4,1)}), s8[4194304]{0:T(1024)(128)(4,1)S(1)}, s32[]{:S(2)}) async-start(s8[6291456]{0:T(1024)(128)(4,1)} %bitcast.174), calls=%async_computation.3 | async-start | bytes 8388608
  79.3 5.2 %copy-start.14 = (bf16[6144,256]{1,0:T(8,128)(2,1)S(1)}, bf16[6144,256]{1,0:T(8,128)(2,1)}, u32[]{:S(2)}) copy-start(bf16[6144,256]{1,0:T(8,128)(2,1)} %copy-done.13) | copy-start | bytes 9437188
  79.3 6.2 %slice-start.1 = ((s8[6291456]{0:T(1024)(128)(4,1)}), s8[2097152]{0:T(1024)(128)(4,1)S(1)}, s32[]{:S(2)}) async-start(s8[6291456]{0:T(1024)(128)(4,1)} %bitcast.174), calls=%async_computation.4 | async-start | bytes 4194304
  85.5 7.3 %copy-start.2 = (bf16[6144,128]{1,0:T(8,128)(2,1)S(1)}, bf16[6144,128]{1,0:T(8,128)(2,1)}, u32[]{:S(2)}) copy-start(bf16[6144,128]{1,0:T(8,128)(2,1)} %copy-done.1) | copy-start | bytes 4718596
  85.5 7.3 %copy-start.4 = (bf16[6144,128]{1,0:T(8,128)(2,1)S(1)}, bf16[6144,128]{1,0:T(8,128)(2,1)}, u32[]{:S(2)}) copy-start(bf16[6144,128]{1,0:T(8,128)(2,1)} %copy-done.3) | copy-start | bytes 4718596
  88.3 6.2 %collective-permute-start.2 = (f32[1540]{0:T(1024)S(1)}, f32[1540]{0:T(1024)S(1)}, u32[]{:S(2)}, u32[]{:S(2)}) collective-permute-start(f32[1540]{0:T(1024)S(1)} %pad_maximum_fusion.6), channel_id=1, source_target_pairs={{0,1},{1,0},{2,3},{3,2},{4,5},{5,4},{6,7},{7,6},{8,9},{9,8},{10,11... | collective-permute-start | bytes 18488 | tf_op jit(solution)/shard_map/ppermute | solution.py:246
  92.8 3.4 %collective-permute-start.1 = (f32[128,256]{1,0:T(8,128)S(1)}, f32[128,256]{1,0:T(8,128)S(1)}, u32[]{:S(2)}, u32[]{:S(2)}) collective-permute-start(f32[128,256]{1,0:T(8,128)S(1)} %constant_dynamic-slice_fusion.1), channel_id=1, source_target_pairs={{0,1},{1,0},{2,3},{3,2},{4,5},{5,4},{6,7},{7,6},{8,9},{9,8},{10,11... | collective-permute-start | bytes 393224 | tf_op jit(solution)/shard_map/ppermute | solution.py:246
  94.0 2.9 %collective-permute-start = (f32[128,256]{1,0:T(8,128)S(1)}, f32[128,256]{1,0:T(8,128)S(1)}, u32[]{:S(2)}, u32[]{:S(2)}) collective-permute-start(f32[128,256]{1,0:T(8,128)S(1)} %constant_dynamic-slice_fusion), channel_id=1, source_target_pairs={{0,1},{1,0},{2,3},{3,2},{4,5},{5,4},{6,7},{7,6},{8,9},{9,8},{10,11... | collective-permute-start | bytes 393224 | tf_op jit(solution)/shard_map/ppermute | solution.py:246
